TPU v7x, 256 devices: a whole 4x4x8 slice. The times are simulated.
256 devices in a mesh: pair: 16 (over z, core), virt: 16 (over x, y).
Axes of the slice: x: 4, y: 4, z: 8, core: 2. Of those that a mesh axis runs over, the one named last changes fastest.
Arguments:
- amplitudes: float32 [64, 2048, 4096], P('virt', 'pair'), may hold values from -0.9 to 0.9
- integrals: float32 [64, 384, 4096], P('virt', 'pair'), may hold values from -0.09375 to 0.09375
- tile_flags: int32 [64], P('virt'), may hold values 0 or 1
- live_count: int32 [16], replicated, may hold values from 1 to 4, as said below
- pair_occ: int32 [2048, 2], P(('pair', 'virt')), may hold values from 0 to 199
- occ_energy: float32 [200], replicated, may hold values from -2.5 to -0.3
- ab_energy: float32 [384], replicated, may hold values from 0.6 to 3
Outputs:
- ladder: float32 [2048, 384], P(('pair', 'virt'))
- update: float32 [2048, 384], P(('pair', 'virt'))
Inputs may be any that keep to these rules, and one draw needn't show every extreme that they name: `live_count`: entry v is how many of the 4 slots of virt index v hold tile pairs: its slots below that number do, and the contents of the others are not to be used. At some index it is 4, and at the index half the axis away it is 1.
All inputs are finite; a program needn't handle non-finite values. No bound on the sum of `tile_flags` on one device may be relied on, other than what follows from the above.
Results may differ from a plain program's by a relative error of at most 0.0001.
Values sent between devices are 32-bit elements; how exact they have to be, the bound alone decides.
No kernel may reach another device: no remote copies, remote signals or barrier semaphores. Data moves between devices by JAX's collectives and lax.ppermute only.
A program may use at most 128 MiB of HBM per device.

v0:
```python
import jax
import jax.numpy as jnp
from jax import lax
from jax.sharding import PartitionSpec as P

TILE = 64


def symmetric_rows(rows, flag):
    shaped = rows.reshape(rows.shape[0], TILE, TILE)
    swapped = jnp.swapaxes(shaped, 1, 2).reshape(rows.shape)
    return rows + flag.astype(jnp.float32) * swapped


def tile_product(amp_tile, int_rows):
    return lax.dot_general(
        amp_tile,
        int_rows,
        (((1,), (1,)), ((), ())),
        precision=lax.Precision.HIGHEST,
        preferred_element_type=jnp.float32,
    )


def on_device(amplitudes, integrals, tile_flags, live_count, pair_occ, occ_energy, ab_energy):
    slots, pair_rows, _ = amplitudes.shape
    virt_index = lax.axis_index("virt")
    n_virt = lax.axis_size("virt")
    own_count = live_count[virt_index]
    running = None
    for slot in range(slots):
        sym_rows = symmetric_rows(integrals[slot], tile_flags[slot])
        gathered = lax.all_gather(sym_rows, "pair", axis=0, tiled=True)
        term = tile_product(amplitudes[slot], gathered)
        term = jnp.where(slot < own_count, term, jnp.zeros_like(term))
        running = term if running is None else running + term
    ab = running.shape[1]
    blocks = running.reshape(n_virt, pair_rows // n_virt, ab)
    received = lax.all_to_all(blocks, "virt", 0, 0, tiled=False)
    ladder = jnp.sum(received, axis=0)
    occ_range = jnp.arange(occ_energy.shape[0], dtype=jnp.int32)
    first_energy = jnp.sum(
        jnp.where(pair_occ[:, 0:1] == occ_range[None, :], occ_energy[None, :], 0.0), axis=1
    )
    second_energy = jnp.sum(
        jnp.where(pair_occ[:, 1:2] == occ_range[None, :], occ_energy[None, :], 0.0), axis=1
    )
    denominator = ab_energy[None, :] - first_energy[:, None] - second_energy[:, None]
    return (ladder, ladder / denominator)


def solution(mesh):
    return jax.shard_map(
        on_device,
        mesh=mesh,
        in_specs=(
            P("virt", "pair", None),
            P("virt", "pair", None),
            P("virt"),
            P(),
            P(("pair", "virt"), None),
            P(),
            P(),
        ),
        out_specs=(P(("pair", "virt"), None), P(("pair", "virt"), None)),
        check_vma=False,
    )
```

profile of v0, /device:TPU:1, one launch (start us, length us, event | category | flops | bytes accessed | tf_op | source)
XLA Modules:
  0.0 243.5 jit_solution(8998881442713806201)
XLA Ops:
  7.2 1.4 fusion.36
  11.1 2.4 slice_multiply_fusion
  13.5 0.3 mul.62
  14.4 0.3 mul.67
  15.0 1.0 mul.69
  16.0 1.3 mul.72
  17.6 1.0 mul.74
  18.7 1.3 mul.77
  20.5 2.4 bitcast_add_fusion
  23.0 0.7 all-gather.9.cloned.1.call-update
  23.7 0.7 all-gather.5.cloned.1.call-update
  24.6 0.3 all-gather.11.cloned.1.call-update
  25.0 0.6 dynamic_slice.3
  28.2 45.1 %all-gather.7.cloned.1.call-done = f32[384,4096]{1,0:T(8,128)} async-done(((f32[24,4096]{1,0:T(8,128)}), f32[384,4096]{1,0:T(8,128)}) %all-gather.7.cloned.1.call-update) | async-done | bytes 6291472 | tf_op jit(solution)/shard_map/all_gather | solution.py:33
  73.3 9.3 %fusion.21 = f32[384,128]{0,1:T(8,128)S(1)} fusion(f32[384,4096]{1,0:T(8,128)} %all-gather.7.cloned.1.call-done, f32[4,128,4096]{2,1,0:T(8,128)} %param.7, pred[]{:T(512)} %bitcast.5), kind=kOutput, calls=%fused_computation.15 | convolution fusion | flops 2415968256 | bytes 8585728 | tf_op jit(solution)/shard_map/dot_general | solution.py:16
  82.6 37.3 %all-gather.9.cloned.1.call-done = f32[384,4096]{1,0:T(8,128)} async-done(((f32[24,4096]{1,0:T(8,128)}), f32[384,4096]{1,0:T(8,128)}) %all-gather.9.cloned.1.call-update) | async-done | bytes 6291472 | tf_op jit(solution)/shard_map/all_gather | solution.py:33
  119.8 9.3 %fusion.24 = f32[384,128]{0,1:T(8,128)S(1)} fusion(f32[384,4096]{1,0:T(8,128)} %all-gather.9.cloned.1.call-done, f32[4,128,4096]{2,1,0:T(8,128)} %param.7, pred[]{:T(512)} %bitcast.10), kind=kOutput, calls=%fused_computation.16 | convolution fusion | flops 2415968256 | bytes 8585728 | tf_op jit(solution)/shard_map/dot_general | solution.py:16
  129.1 37.3 %all-gather.5.cloned.1.call-done = f32[384,4096]{1,0:T(8,128)} async-done(((f32[24,4096]{1,0:T(8,128)}), f32[384,4096]{1,0:T(8,128)}) %all-gather.5.cloned.1.call-update) | async-done | bytes 6291472 | tf_op jit(solution)/shard_map/all_gather | solution.py:33
  166.4 9.5 %fusion.18 = f32[384,128]{0,1:T(8,128)S(1)} fusion(f32[384,128]{0,1:T(8,128)S(1)} %fusion.24, f32[384,128]{0,1:T(8,128)S(1)} %fusion.21, f32[384,4096]{1,0:T(8,128)} %all-gather.5.cloned.1.call-done, f32[4,128,4096]{2,1,0:T(8,128)} %param.7, pred[]{:T(512)} %bitcast), kind=kOutput, calls=%fused_computation.14 | convolution fusion | flops 2416066560 | bytes 8978944 | tf_op jit(solution)/shard_map/dot_general | solution.py:16
  175.9 36.8 %all-gather.11.cloned.1.call-done = f32[384,4096]{1,0:T(8,128)} async-done(((f32[24,4096]{1,0:T(8,128)}), f32[384,4096]{1,0:T(8,128)}) %all-gather.11.cloned.1.call-update) | async-done | bytes 6291472 | tf_op jit(solution)/shard_map/all_gather | solution.py:33
  212.8 9.9 %fusion.33 = f32[16,8,384]{2,1,0:T(8,128)} fusion(f32[384,128]{0,1:T(8,128)S(1)} %fusion.18, f32[384,4096]{1,0:T(8,128)} %all-gather.11.cloned.1.call-done, f32[4,128,4096]{2,1,0:T(8,128)} %param.7, pred[]{:T(512)} %bitcast.15), kind=kOutput, calls=%fused_computation.19 | convolution fusion | flops 2416017408 | bytes 8782336 | tf_op jit(solution)/shard_map/dot_general | solution.py:16
  222.7 6.5 %all-to-all-start = ((f32[16,8,384]{2,1,0:T(8,128)}), f32[16,8,384]{2,1,0:T(8,128)S(1)}, u32[]{:S(2)}, u32[]{:S(2)}) async-start(f32[16,8,384]{2,1,0:T(8,128)} %fusion.33), calls=%async_computation | async-start | bytes 393216 | tf_op jit(solution)/shard_map/all_to_all | solution.py:39
  229.5 6.8 %all-to-all-done = f32[16,8,384]{2,1,0:T(8,128)S(1)} async-done(((f32[16,8,384]{2,1,0:T(8,128)}), f32[16,8,384]{2,1,0:T(8,128)S(1)}, u32[]{:S(2)}, u32[]{:S(2)}) %all-to-all-start) | async-done | bytes 196640 | tf_op jit(solution)/shard_map/all_to_all | solution.py:39
  236.3 0.7 subtract_divide_fusion
  (26 shorter events, 2.3 us)
Async XLA Ops:
  7.2 66.1 %all-gather.7.cloned.1.call-start = ((), (), s32[]{:S(2)}) async-start(), calls=%async_computation.2 | async-start | bytes 6684672 | tf_op jit(solution)/shard_map/all_gather | solution.py:33
  14.1 6.4 %copy-start = (f32[4,24,4096]{2,1,0:T(8,128)S(1)}, f32[4,24,4096]{2,1,0:T(8,128)}, u32[]{:S(2)}) copy-start(f32[4,24,4096]{2,1,0:T(8,128)} %param.8) | copy-start | bytes 4718596
  17.3 7.7 %copy-start.5 = (s32[16]{0:T(128)S(1)}, s32[16]{0:T(128)}, u32[]{:S(2)}) copy-start(s32[16]{0:T(128)} %param.10) | copy-start | bytes 196
  22.9 96.9 %all-gather.9.cloned.1.call-start = ((), (), s32[]{:S(2)}) async-start(), calls=%async_computation.3 | async-start | bytes 6684672 | tf_op jit(solution)/shard_map/all_gather | solution.py:33
  23.7 142.7 %all-gather.5.cloned.1.call-start = ((), (), s32[]{:S(2)}) async-start(), calls=%async_computation.1 | async-start | bytes 6684672 | tf_op jit(solution)/shard_map/all_gather | solution.py:33
  24.4 188.3 %all-gather.11.cloned.1.call-start = ((), (), s32[]{:S(2)}) async-start(), calls=%async_computation.4 | async-start | bytes 6684672 | tf_op jit(solution)/shard_map/all_gather | solution.py:33
  175.9 53.4 %copy-start.4 = (s32[8,2]{0,1:T(2,128)S(1)}, s32[8,2]{0,1:T(2,128)}, u32[]{:S(2)}) copy-start(s32[8,2]{0,1:T(2,128)} %param.11) | copy-start | bytes 196
  175.9 53.4 %copy-start.3 = (f32[200]{0:T(256)S(1)}, f32[200]{0:T(256)}, u32[]{:S(2)}) copy-start(f32[200]{0:T(256)} %param.12) | copy-start | bytes 2404
  175.9 60.4 %copy-start.2 = (f32[384]{0:T(512)S(1)}, f32[384]{0:T(512)}, u32[]{:S(2)}) copy-start(f32[384]{0:T(512)} %param.13) | copy-start | bytes 4612
  222.7 13.5 %all-to-all-start = ((f32[16,8,384]{2,1,0:T(8,128)}), f32[16,8,384]{2,1,0:T(8,128)S(1)}, u32[]{:S(2)}, u32[]{:S(2)}) async-start(f32[16,8,384]{2,1,0:T(8,128)} %fusion.33), calls=%async_computation | async-start | bytes 393216 | tf_op jit(solution)/shard_map/all_to_all | solution.py:39
  236.3 0.7 copy-start.1
Sparse Core Ops, SparseCore 0:
  23.0 50.2 all-gather.6
  75.1 44.6 all-gather.8
  121.7 44.6 all-gather.4
  168.1 44.6 all-gather.10
where the time goes:
time: 244 us; the launch traced here: 243 us
  waiting for transfers between devices  165 us (68%)
  matrix products  38 us (16%)
  between operations  19 us (8%)
  local copies, waits for them, and re-layouts  8.98 us (4%)
  starting transfers between devices  6.86 us (3%)
  other arithmetic  5.67 us (2%)
    all_gather x4, waiting for transfers between devices, on_device(): gathered = lax.all_gather(sym_rows, 'pair', axis=0, tiled=True)  157 us
    dot_general x4, matrix products, tile_product(): lax.dot_general(amp_tile, int_rows, (((1,), (1,)), ((), ())), precision=l...  38 us
    mul x12, local copies, waits for them, and re-layouts, symmetric_rows(): return rows + flag.astype(jnp.float32) * swapped  6.94 us
    all_to_all x1, waiting for transfers between devices, on_device(): received = lax.all_to_all(blocks, 'virt', 0, 0, tiled=False)  6.75 us
    all_to_all x1, starting transfers between devices, on_device(): received = lax.all_to_all(blocks, 'virt', 0, 0, tiled=False)  6.52 us
  transfers between devices with their start and end apart: 5, of which 5 were waited for; matrix products, arithmetic and copies ran while one was open for 12% of the time, Pallas kernels for 0%

commit v1 on v0

--- a/solution.py
+++ b/solution.py
@@ -30,7 +30,25 @@
     running = None
     for slot in range(slots):
         sym_rows = symmetric_rows(integrals[slot], tile_flags[slot])
-        gathered = lax.all_gather(sym_rows, "pair", axis=0, tiled=True)
+        ways, here, step = (lax.axis_size("pair"), lax.axis_index("pair"), sym_rows.shape[0])
+        shape = [n * ways if d == 0 else n for d, n in enumerate(sym_rows.shape)]
+        full = lax.dynamic_update_slice_in_dim(
+            jnp.zeros(shape, sym_rows.dtype), sym_rows, here * step, axis=0
+        )
+        going_up = going_down = sym_rows
+        for far in range(1, ways // 2 + 1):
+            going_up = lax.ppermute(going_up, "pair", [(d, (d + 1) % ways) for d in range(ways)])
+            full = lax.dynamic_update_slice_in_dim(
+                full, going_up, (here - far) % ways * step, axis=0
+            )
+            if 2 * far < ways:
+                going_down = lax.ppermute(
+                    going_down, "pair", [(d, (d - 1) % ways) for d in range(ways)]
+                )
+                full = lax.dynamic_update_slice_in_dim(
+                    full, going_down, (here + far) % ways * step, axis=0
+                )
+        gathered = full
         term = tile_product(amplitudes[slot], gathered)
         term = jnp.where(slot < own_count, term, jnp.zeros_like(term))
         running = term if running is None else running + term

time: 244 us -> 221 us (0.906)
  the two profiles are of different devices: /device:TPU:1 before, /device:TPU:2 now
where the time goes in v1:
time: 221 us
  starting transfers between devices  92.6 us (42%)
  local copies, waits for them, and re-layouts  71.2 us (32%)
  matrix products  32.6 us (15%)
  waiting for transfers between devices  11 us (5%)
  other arithmetic  7.1 us (3%)
  between operations  6.17 us (3%)
    ppermute x28, starting transfers between devices, on_device(): lax.ppermute(going_down, 'pair', [(d, (d - 1) % ways) for d in range(ways)])  85 us
    dot_general x4, matrix products, tile_product(): lax.dot_general(amp_tile, int_rows, (((1,), (1,)), ((), ())), precision=l...  32.6 us
    dynamic_update_slice x32, local copies, waits for them, and re-layouts, on_device(): lax.dynamic_update_slice_in_dim(full, going_up, (here - far) % ways * ste...  28.2 us
    dynamic_update_slice x28, local copies, waits for them, and re-layouts, on_device(): lax.dynamic_update_slice_in_dim(full, going_down, (here + far) % ways * s...  23.9 us
    another operation x4, local copies, waits for them, and re-layouts  13.6 us
    all_to_all x1, starting transfers between devices, on_device(): received = lax.all_to_all(blocks, 'virt', 0, 0, tiled=False)  7.48 us
    all_to_all x1, waiting for transfers between devices, on_device(): received = lax.all_to_all(blocks, 'virt', 0, 0, tiled=False)  6.34 us
    ppermute x32, waiting for transfers between devices, on_device(): lax.ppermute(going_up, 'pair', [(d, (d + 1) % ways) for d in range(ways)])  4.57 us
  transfers between devices with their start and end apart: 61, of which 3 were waited for; matrix products, arithmetic and copies ran while one was open for 42% of the time, Pallas kernels for 0%

profile of v1, /device:TPU:2, one launch (start us, length us, event | category | flops | bytes accessed | tf_op | source)
XLA Modules:
  0.0 220.6 jit_solution(18061038503843737480)
XLA Ops:
  8.0 3.4 %broadcast.62.clone = f32[384,4096]{1,0:T(8,128)} broadcast(f32[]{:T(128)} %constant.191.clone.1), dimensions={} | broadcast | bytes 6291460 | tf_op jit(solution)/shard_map/broadcast.3
  12.4 5.3 %collective-permute-start.46 = (f32[24,4096]{1,0:T(8,128)}, f32[24,4096]{1,0:T(8,128)}, u32[]{:S(2)}, u32[]{:S(2)}) collective-permute-start(f32[24,4096]{1,0:T(8,128)} %get-tuple-element.11), channel_id=1, source_target_pairs={{0,240},{16,0},{32,16},{48,32},{64,48},{80,64},{96,80},{112,96},{1... | collective-permute-start | bytes 1179656 | tf_op jit(solution)/shard_map/ppermute | solution.py:45
  18.6 3.5 %broadcast.62.clone.1 = f32[384,4096]{1,0:T(8,128)} broadcast(f32[]{:T(128)} %constant.191.clone.1), dimensions={} | broadcast | bytes 6291460 | tf_op jit(solution)/shard_map/broadcast.3
  23.0 3.0 %collective-permute-start.31 = (f32[24,4096]{1,0:T(8,128)}, f32[24,4096]{1,0:T(8,128)}, u32[]{:S(2)}, u32[]{:S(2)}) collective-permute-start(f32[24,4096]{1,0:T(8,128)} %get-tuple-element.9), channel_id=1, source_target_pairs={{0,240},{16,0},{32,16},{48,32},{64,48},{80,64},{96,80},{112,96},{1... | collective-permute-start | bytes 1179656 | tf_op jit(solution)/shard_map/ppermute | solution.py:45
  26.8 3.3 %broadcast.62.clone.2 = f32[384,4096]{1,0:T(8,128)} broadcast(f32[]{:T(128)} %constant.191.clone.1), dimensions={} | broadcast | bytes 6291460 | tf_op jit(solution)/shard_map/broadcast.3
  32.0 3.4 %broadcast.62.clone.3 = f32[384,4096]{1,0:T(8,128)} broadcast(f32[]{:T(128)} %constant.191.clone.1), dimensions={} | broadcast | bytes 6291460 | tf_op jit(solution)/shard_map/broadcast.3
  39.5 3.0 %collective-permute-start.16 = (f32[24,4096]{1,0:T(8,128)}, f32[24,4096]{1,0:T(8,128)S(1)}, u32[]{:S(2)}, u32[]{:S(2)}) collective-permute-start(f32[24,4096]{1,0:T(8,128)} %get-tuple-element.7), channel_id=1, source_target_pairs={{0,240},{16,0},{32,16},{48,32},{64,48},{80,64},{96,80},{112,96},{1... | collective-permute-start | bytes 1179656 | tf_op jit(solution)/shard_map/ppermute | solution.py:45
  46.1 3.0 %collective-permute-start.1 = (f32[24,4096]{1,0:T(8,128)S(1)}, f32[24,4096]{1,0:T(8,128)S(1)}, u32[]{:S(2)}, u32[]{:S(2)}) collective-permute-start(f32[24,4096]{1,0:T(8,128)S(1)} %get-tuple-element.5), channel_id=1, source_target_pairs={{0,240},{16,0},{32,16},{48,32},{64,48},{80,64},{96,80},{112,96},{1... | collective-permute-start | bytes 1179656 | tf_op jit(solution)/shard_map/ppermute | solution.py:45
  62.6 3.0 %collective-permute-start.18 = (f32[24,4096]{1,0:T(8,128)S(1)}, f32[24,4096]{1,0:T(8,128)S(1)}, u32[]{:S(2)}, u32[]{:S(2)}) collective-permute-start(f32[24,4096]{1,0:T(8,128)S(1)} %collective-permute-done.16), channel_id=1, source_target_pairs={{0,240},{16,0},{32,16},{48,32},{64,48},{80,64},{96,80},{112,96},{1... | collective-permute-start | bytes 1179656 | tf_op jit(solution)/shard_map/ppermute | solution.py:45
  85.3 2.9 %collective-permute-start.5 = (f32[24,4096]{1,0:T(8,128)S(1)}, f32[24,4096]{1,0:T(8,128)S(1)}, u32[]{:S(2)}, u32[]{:S(2)}) collective-permute-start(f32[24,4096]{1,0:T(8,128)S(1)} %collective-permute-done.3), channel_id=1, source_target_pairs={{0,240},{16,0},{32,16},{48,32},{64,48},{80,64},{96,80},{112,96},{1... | collective-permute-start | bytes 1179656 | tf_op jit(solution)/shard_map/ppermute | solution.py:45
  89.8 3.0 %collective-permute-start.52 = (f32[24,4096]{1,0:T(8,128)S(1)}, f32[24,4096]{1,0:T(8,128)S(1)}, u32[]{:S(2)}, u32[]{:S(2)}) collective-permute-start(f32[24,4096]{1,0:T(8,128)S(1)} %collective-permute-done.50), channel_id=1, source_target_pairs={{0,240},{16,0},{32,16},{48,32},{64,48},{80,64},{96,80},{112,96},{1... | collective-permute-start | bytes 1179656 | tf_op jit(solution)/shard_map/ppermute | solution.py:45
  94.3 3.0 %collective-permute-start.37 = (f32[24,4096]{1,0:T(8,128)S(1)}, f32[24,4096]{1,0:T(8,128)S(1)}, u32[]{:S(2)}, u32[]{:S(2)}) collective-permute-start(f32[24,4096]{1,0:T(8,128)S(1)} %collective-permute-done.35), channel_id=1, source_target_pairs={{0,240},{16,0},{32,16},{48,32},{64,48},{80,64},{96,80},{112,96},{1... | collective-permute-start | bytes 1179656 | tf_op jit(solution)/shard_map/ppermute | solution.py:45
  117.1 2.9 %collective-permute-start.24 = (f32[24,4096]{1,0:T(8,128)S(1)}, f32[24,4096]{1,0:T(8,128)S(1)}, u32[]{:S(2)}, u32[]{:S(2)}) collective-permute-start(f32[24,4096]{1,0:T(8,128)S(1)} %collective-permute-done.22), channel_id=1, source_target_pairs={{0,240},{16,0},{32,16},{48,32},{64,48},{80,64},{96,80},{112,96},{1... | collective-permute-start | bytes 1179656 | tf_op jit(solution)/shard_map/ppermute | solution.py:45
  126.1 3.0 %collective-permute-start.56 = (f32[24,4096]{1,0:T(8,128)S(1)}, f32[24,4096]{1,0:T(8,128)S(1)}, u32[]{:S(2)}, u32[]{:S(2)}) collective-permute-start(f32[24,4096]{1,0:T(8,128)S(1)} %collective-permute-done.54), channel_id=1, source_target_pairs={{0,240},{16,0},{32,16},{48,32},{64,48},{80,64},{96,80},{112,96},{1... | collective-permute-start | bytes 1179656 | tf_op jit(solution)/shard_map/ppermute | solution.py:45
  135.2 3.0 %collective-permute-start.26 = (f32[24,4096]{1,0:T(8,128)S(1)}, f32[24,4096]{1,0:T(8,128)S(1)}, u32[]{:S(2)}, u32[]{:S(2)}) collective-permute-start(f32[24,4096]{1,0:T(8,128)S(1)} %collective-permute-done.24), channel_id=1, source_target_pairs={{0,240},{16,0},{32,16},{48,32},{64,48},{80,64},{96,80},{112,96},{1... | collective-permute-start | bytes 1179656 | tf_op jit(solution)/shard_map/ppermute | solution.py:45
  139.7 3.0 %collective-permute-start.11 = (f32[24,4096]{1,0:T(8,128)S(1)}, f32[24,4096]{1,0:T(8,128)S(1)}, u32[]{:S(2)}, u32[]{:S(2)}) collective-permute-start(f32[24,4096]{1,0:T(8,128)S(1)} %collective-permute-done.9), channel_id=1, source_target_pairs={{0,240},{16,0},{32,16},{48,32},{64,48},{80,64},{96,80},{112,96},{1... | collective-permute-start | bytes 1179656 | tf_op jit(solution)/shard_map/ppermute | solution.py:45
  153.3 2.9 %collective-permute-start.28 = (f32[24,4096]{1,0:T(8,128)S(1)}, f32[24,4096]{1,0:T(8,128)S(1)}, u32[]{:S(2)}, u32[]{:S(2)}) collective-permute-start(f32[24,4096]{1,0:T(8,128)S(1)} %collective-permute-done.26), channel_id=1, source_target_pairs={{0,240},{16,0},{32,16},{48,32},{64,48},{80,64},{96,80},{112,96},{1... | collective-permute-start | bytes 1179656 | tf_op jit(solution)/shard_map/ppermute | solution.py:45
  157.8 3.0 %collective-permute-start.13 = (f32[24,4096]{1,0:T(8,128)S(1)}, f32[24,4096]{1,0:T(8,128)S(1)}, u32[]{:S(2)}, u32[]{:S(2)}) collective-permute-start(f32[24,4096]{1,0:T(8,128)S(1)} %collective-permute-done.11), channel_id=1, source_target_pairs={{0,240},{16,0},{32,16},{48,32},{64,48},{80,64},{96,80},{112,96},{1... | collective-permute-start | bytes 1179656 | tf_op jit(solution)/shard_map/ppermute | solution.py:45
  170.8 8.1 %fusion.27 = f32[384,128]{0,1:T(8,128)S(1)} fusion(f32[384,4096]{1,0:T(8,128)} %constant_dynamic-update-slice_fusion, f32[4,128,4096]{2,1,0:T(8,128)S(1)} %bitcast.65, pred[]{:T(512)} %bitcast.15), kind=kOutput, calls=%fused_computation.17 | convolution fusion | flops 2415968256 | bytes 8585217 | tf_op jit(solution)/shard_map/dot_general | solution.py:16
  179.7 7.9 %fusion.24 = f32[384,128]{0,1:T(8,128)S(1)} fusion(f32[384,4096]{1,0:T(8,128)} %constant_dynamic-update-slice_fusion.16, f32[4,128,4096]{2,1,0:T(8,128)S(1)} %bitcast.65, pred[]{:T(512)} %bitcast.10), kind=kOutput, calls=%fused_computation.16 | convolution fusion | flops 2415968256 | bytes 8585217 | tf_op jit(solution)/shard_map/dot_general | solution.py:16
  188.5 7.9 %fusion.21 = f32[384,128]{0,1:T(8,128)S(1)} fusion(f32[384,4096]{1,0:T(8,128)} %constant_dynamic-update-slice_fusion.32, f32[4,128,4096]{2,1,0:T(8,128)S(1)} %bitcast.65, pred[]{:T(512)} %bitcast.5), kind=kOutput, calls=%fused_computation.15 | convolution fusion | flops 2415968256 | bytes 8585217 | tf_op jit(solution)/shard_map/dot_general | solution.py:16
  197.2 8.6 %fusion.33 = f32[16,8,384]{2,1,0:T(8,128)} fusion(f32[384,128]{0,1:T(8,128)S(1)} %fusion.27, f32[384,128]{0,1:T(8,128)S(1)} %fusion.24, f32[384,128]{0,1:T(8,128)S(1)} %fusion.21, f32[384,4096]{1,0:T(8,128)} %constant_dynamic-update-slice_fusion.48, f32[4,128,4096]{2,1,0:T(8,128)S(1)} %bitcast.65, pred[]{:T(512)} %bitcast), kind=kOutput, calls=%fused_computation.19 | convolution fusion | flops 2416115712 | bytes 9175041 | tf_op jit(solution)/shard_map/dot_general | solution.py:16
  205.8 7.5 %all-to-all-start = ((f32[16,8,384]{2,1,0:T(8,128)}), f32[16,8,384]{2,1,0:T(8,128)S(1)}, u32[]{:S(2)}, u32[]{:S(2)}) async-start(f32[16,8,384]{2,1,0:T(8,128)} %fusion.33), calls=%async_computation | async-start | bytes 393216 | tf_op jit(solution)/shard_map/all_to_all | solution.py:57
  213.6 6.3 %all-to-all-done = f32[16,8,384]{2,1,0:T(8,128)S(1)} async-done(((f32[16,8,384]{2,1,0:T(8,128)}), f32[16,8,384]{2,1,0:T(8,128)S(1)}, u32[]{:S(2)}, u32[]{:S(2)}) %all-to-all-start) | async-done | bytes 196640 | tf_op jit(solution)/shard_map/all_to_all | solution.py:57
  (210 shorter events, 110.5 us)
Async XLA Ops:
  12.4 27.1 %collective-permute-start.45 = (f32[24,4096]{1,0:T(8,128)}, f32[24,4096]{1,0:T(8,128)}, u32[]{:S(2)}, u32[]{:S(2)}) collective-permute-start(f32[24,4096]{1,0:T(8,128)} %get-tuple-element.11), channel_id=1, source_target_pairs={{0,16},{16,32},{32,48},{48,64},{64,80},{80,96},{96,112},{112,128},... | collective-permute-start | bytes 1179656 | tf_op jit(solution)/shard_map/ppermute | solution.py:40
  12.4 33.7 %collective-permute-start.46 = (f32[24,4096]{1,0:T(8,128)}, f32[24,4096]{1,0:T(8,128)}, u32[]{:S(2)}, u32[]{:S(2)}) collective-permute-start(f32[24,4096]{1,0:T(8,128)} %get-tuple-element.11), channel_id=1, source_target_pairs={{0,240},{16,0},{32,16},{48,32},{64,48},{80,64},{96,80},{112,96},{1... | collective-permute-start | bytes 1179656 | tf_op jit(solution)/shard_map/ppermute | solution.py:45
  23.0 21.3 %collective-permute-start.30 = (f32[24,4096]{1,0:T(8,128)}, f32[24,4096]{1,0:T(8,128)}, u32[]{:S(2)}, u32[]{:S(2)}) collective-permute-start(f32[24,4096]{1,0:T(8,128)} %get-tuple-element.9), channel_id=1, source_target_pairs={{0,16},{16,32},{32,48},{48,64},{64,80},{80,96},{96,112},{112,128},... | collective-permute-start | bytes 1179656 | tf_op jit(solution)/shard_map/ppermute | solution.py:40
  23.0 27.9 %collective-permute-start.31 = (f32[24,4096]{1,0:T(8,128)}, f32[24,4096]{1,0:T(8,128)}, u32[]{:S(2)}, u32[]{:S(2)}) collective-permute-start(f32[24,4096]{1,0:T(8,128)} %get-tuple-element.9), channel_id=1, source_target_pairs={{0,240},{16,0},{32,16},{48,32},{64,48},{80,64},{96,80},{112,96},{1... | collective-permute-start | bytes 1179656 | tf_op jit(solution)/shard_map/ppermute | solution.py:45
  31.1 21.5 %collective-permute-start.15 = (f32[24,4096]{1,0:T(8,128)}, f32[24,4096]{1,0:T(8,128)}, u32[]{:S(2)}, u32[]{:S(2)}) collective-permute-start(f32[24,4096]{1,0:T(8,128)} %get-tuple-element.7), channel_id=1, source_target_pairs={{0,16},{16,32},{32,48},{48,64},{64,80},{80,96},{96,112},{112,128},... | collective-permute-start | bytes 1179656 | tf_op jit(solution)/shard_map/ppermute | solution.py:40
  39.5 17.8 %collective-permute-start.16 = (f32[24,4096]{1,0:T(8,128)}, f32[24,4096]{1,0:T(8,128)S(1)}, u32[]{:S(2)}, u32[]{:S(2)}) collective-permute-start(f32[24,4096]{1,0:T(8,128)} %get-tuple-element.7), channel_id=1, source_target_pairs={{0,240},{16,0},{32,16},{48,32},{64,48},{80,64},{96,80},{112,96},{1... | collective-permute-start | bytes 1179656 | tf_op jit(solution)/shard_map/ppermute | solution.py:45
  44.3 13.8 %collective-permute-start = (f32[24,4096]{1,0:T(8,128)S(1)}, f32[24,4096]{1,0:T(8,128)S(1)}, u32[]{:S(2)}, u32[]{:S(2)}) collective-permute-start(f32[24,4096]{1,0:T(8,128)S(1)} %get-tuple-element.5), channel_id=1, source_target_pairs={{0,16},{16,32},{32,48},{48,64},{64,80},{80,96},{96,112},{112,128},... | collective-permute-start | bytes 1179656 | tf_op jit(solution)/shard_map/ppermute | solution.py:40
  46.1 15.8 %collective-permute-start.1 = (f32[24,4096]{1,0:T(8,128)S(1)}, f32[24,4096]{1,0:T(8,128)S(1)}, u32[]{:S(2)}, u32[]{:S(2)}) collective-permute-start(f32[24,4096]{1,0:T(8,128)S(1)} %get-tuple-element.5), channel_id=1, source_target_pairs={{0,240},{16,0},{32,16},{48,32},{64,48},{80,64},{96,80},{112,96},{1... | collective-permute-start | bytes 1179656 | tf_op jit(solution)/shard_map/ppermute | solution.py:45
  52.6 14.6 %collective-permute-start.48 = (f32[24,4096]{1,0:T(8,128)}, f32[24,4096]{1,0:T(8,128)S(1)}, u32[]{:S(2)}, u32[]{:S(2)}) collective-permute-start(f32[24,4096]{1,0:T(8,128)} %collective-permute-done.46), channel_id=1, source_target_pairs={{0,240},{16,0},{32,16},{48,32},{64,48},{80,64},{96,80},{112,96},{1... | collective-permute-start | bytes 1179656 | tf_op jit(solution)/shard_map/ppermute | solution.py:45
  58.1 12.8 %collective-permute-start.33 = (f32[24,4096]{1,0:T(8,128)}, f32[24,4096]{1,0:T(8,128)S(1)}, u32[]{:S(2)}, u32[]{:S(2)}) collective-permute-start(f32[24,4096]{1,0:T(8,128)} %collective-permute-done.31), channel_id=1, source_target_pairs={{0,240},{16,0},{32,16},{48,32},{64,48},{80,64},{96,80},{112,96},{1... | collective-permute-start | bytes 1179656 | tf_op jit(solution)/shard_map/ppermute | solution.py:45
  62.6 12.8 %collective-permute-start.18 = (f32[24,4096]{1,0:T(8,128)S(1)}, f32[24,4096]{1,0:T(8,128)S(1)}, u32[]{:S(2)}, u32[]{:S(2)}) collective-permute-start(f32[24,4096]{1,0:T(8,128)S(1)} %collective-permute-done.16), channel_id=1, source_target_pairs={{0,240},{16,0},{32,16},{48,32},{64,48},{80,64},{96,80},{112,96},{1... | collective-permute-start | bytes 1179656 | tf_op jit(solution)/shard_map/ppermute | solution.py:45
  71.8 13.5 %collective-permute-start.50 = (f32[24,4096]{1,0:T(8,128)S(1)}, f32[24,4096]{1,0:T(8,128)S(1)}, u32[]{:S(2)}, u32[]{:S(2)}) collective-permute-start(f32[24,4096]{1,0:T(8,128)S(1)} %collective-permute-done.48), channel_id=1, source_target_pairs={{0,240},{16,0},{32,16},{48,32},{64,48},{80,64},{96,80},{112,96},{1... | collective-permute-start | bytes 1179656 | tf_op jit(solution)/shard_map/ppermute | solution.py:45
  85.3 12.8 %collective-permute-start.5 = (f32[24,4096]{1,0:T(8,128)S(1)}, f32[24,4096]{1,0:T(8,128)S(1)}, u32[]{:S(2)}, u32[]{:S(2)}) collective-permute-start(f32[24,4096]{1,0:T(8,128)S(1)} %collective-permute-done.3), channel_id=1, source_target_pairs={{0,240},{16,0},{32,16},{48,32},{64,48},{80,64},{96,80},{112,96},{1... | collective-permute-start | bytes 1179656 | tf_op jit(solution)/shard_map/ppermute | solution.py:45
  89.8 13.6 %collective-permute-start.52 = (f32[24,4096]{1,0:T(8,128)S(1)}, f32[24,4096]{1,0:T(8,128)S(1)}, u32[]{:S(2)}, u32[]{:S(2)}) collective-permute-start(f32[24,4096]{1,0:T(8,128)S(1)} %collective-permute-done.50), channel_id=1, source_target_pairs={{0,240},{16,0},{32,16},{48,32},{64,48},{80,64},{96,80},{112,96},{1... | collective-permute-start | bytes 1179656 | tf_op jit(solution)/shard_map/ppermute | solution.py:45
  94.3 12.9 %collective-permute-start.37 = (f32[24,4096]{1,0:T(8,128)S(1)}, f32[24,4096]{1,0:T(8,128)S(1)}, u32[]{:S(2)}, u32[]{:S(2)}) collective-permute-start(f32[24,4096]{1,0:T(8,128)S(1)} %collective-permute-done.35), channel_id=1, source_target_pairs={{0,240},{16,0},{32,16},{48,32},{64,48},{80,64},{96,80},{112,96},{1... | collective-permute-start | bytes 1179656 | tf_op jit(solution)/shard_map/ppermute | solution.py:45
  108.0 13.6 %collective-permute-start.54 = (f32[24,4096]{1,0:T(8,128)S(1)}, f32[24,4096]{1,0:T(8,128)S(1)}, u32[]{:S(2)}, u32[]{:S(2)}) collective-permute-start(f32[24,4096]{1,0:T(8,128)S(1)} %collective-permute-done.52), channel_id=1, source_target_pairs={{0,240},{16,0},{32,16},{48,32},{64,48},{80,64},{96,80},{112,96},{1... | collective-permute-start | bytes 1179656 | tf_op jit(solution)/shard_map/ppermute | solution.py:45
  117.1 12.8 %collective-permute-start.24 = (f32[24,4096]{1,0:T(8,128)S(1)}, f32[24,4096]{1,0:T(8,128)S(1)}, u32[]{:S(2)}, u32[]{:S(2)}) collective-permute-start(f32[24,4096]{1,0:T(8,128)S(1)} %collective-permute-done.22), channel_id=1, source_target_pairs={{0,240},{16,0},{32,16},{48,32},{64,48},{80,64},{96,80},{112,96},{1... | collective-permute-start | bytes 1179656 | tf_op jit(solution)/shard_map/ppermute | solution.py:45
  126.1 13.6 %collective-permute-start.56 = (f32[24,4096]{1,0:T(8,128)S(1)}, f32[24,4096]{1,0:T(8,128)S(1)}, u32[]{:S(2)}, u32[]{:S(2)}) collective-permute-start(f32[24,4096]{1,0:T(8,128)S(1)} %collective-permute-done.54), channel_id=1, source_target_pairs={{0,240},{16,0},{32,16},{48,32},{64,48},{80,64},{96,80},{112,96},{1... | collective-permute-start | bytes 1179656 | tf_op jit(solution)/shard_map/ppermute | solution.py:45
  144.3 13.6 %collective-permute-start.58 = (f32[24,4096]{1,0:T(8,128)S(1)}, f32[24,4096]{1,0:T(8,128)S(1)}, u32[]{:S(2)}, u32[]{:S(2)}) collective-permute-start(f32[24,4096]{1,0:T(8,128)S(1)} %collective-permute-done.56), channel_id=1, source_target_pairs={{0,240},{16,0},{32,16},{48,32},{64,48},{80,64},{96,80},{112,96},{1... | collective-permute-start | bytes 1179656 | tf_op jit(solution)/shard_map/ppermute | solution.py:45
  153.3 12.9 %collective-permute-start.28 = (f32[24,4096]{1,0:T(8,128)S(1)}, f32[24,4096]{1,0:T(8,128)S(1)}, u32[]{:S(2)}, u32[]{:S(2)}) collective-permute-start(f32[24,4096]{1,0:T(8,128)S(1)} %collective-permute-done.26), channel_id=1, source_target_pairs={{0,240},{16,0},{32,16},{48,32},{64,48},{80,64},{96,80},{112,96},{1... | collective-permute-start | bytes 1179656 | tf_op jit(solution)/shard_map/ppermute | solution.py:45
  162.4 16.6 %collective-permute-start.44 = (f32[24,4096]{1,0:T(8,128)S(1)}, f32[24,4096]{1,0:T(8,128)S(1)}, u32[]{:S(2)}, u32[]{:S(2)}) collective-permute-start(f32[24,4096]{1,0:T(8,128)S(1)} %collective-permute-done.42), channel_id=1, source_target_pairs={{0,16},{16,32},{32,48},{48,64},{64,80},{80,96},{96,112},{112,128},... | collective-permute-start | bytes 1179656 | tf_op jit(solution)/shard_map/ppermute | solution.py:40
  165.5 22.2 %collective-permute-start.29 = (f32[24,4096]{1,0:T(8,128)S(1)}, f32[24,4096]{1,0:T(8,128)S(1)}, u32[]{:S(2)}, u32[]{:S(2)}) collective-permute-start(f32[24,4096]{1,0:T(8,128)S(1)} %collective-permute-done.27), channel_id=1, source_target_pairs={{0,16},{16,32},{32,48},{48,64},{64,80},{80,96},{96,112},{112,128},... | collective-permute-start | bytes 1179656 | tf_op jit(solution)/shard_map/ppermute | solution.py:40
  166.2 30.2 %collective-permute-start.14 = (f32[24,4096]{1,0:T(8,128)S(1)}, f32[24,4096]{1,0:T(8,128)S(1)}, u32[]{:S(2)}, u32[]{:S(2)}) collective-permute-start(f32[24,4096]{1,0:T(8,128)S(1)} %collective-permute-done.12), channel_id=1, source_target_pairs={{0,16},{16,32},{32,48},{48,64},{64,80},{80,96},{96,112},{112,128},... | collective-permute-start | bytes 1179656 | tf_op jit(solution)/shard_map/ppermute | solution.py:40
  205.8 14.1 %all-to-all-start = ((f32[16,8,384]{2,1,0:T(8,128)}), f32[16,8,384]{2,1,0:T(8,128)S(1)}, u32[]{:S(2)}, u32[]{:S(2)}) async-start(f32[16,8,384]{2,1,0:T(8,128)} %fusion.33), calls=%async_computation | async-start | bytes 393216 | tf_op jit(solution)/shard_map/all_to_all | solution.py:57
  (47 other events, 536.9 us)
